TPU v7x, 512 devices: a whole 4x8x8 slice. The times are simulated.
512 devices in a mesh: dp: 64 (over z, x, core), mp: 8 (over y).
Axes of the slice: x: 4, y: 8, z: 8, core: 2. Of those that a mesh axis runs over, the one named last changes fastest.
Arguments:
- micro_grads: bfloat16 [64, 2, 768, 768], P('dp', None, None, 'mp'), may hold values from -16 to 16
- master: float32 [768, 768], P('dp', 'mp'), may hold values from -0.21875 to 0.21875
- moment: float32 [768, 768], P('dp', 'mp'), may hold values from -1.5 to 1.5
- second: float32 [768, 768], P('dp', 'mp'), may hold values from 0.001 to 0.1
- left_basis: float32 [768, 768], P(None, 'dp'), may hold values from -0.21875 to 0.21875
- right_basis: float32 [768, 768], P(None, 'mp'), may hold values from -0.21875 to 0.21875
- left_stat: float32 [768, 768], P('mp'), may hold values from -2 to 5, as said below
- right_stat: float32 [768, 768], P('mp'), may hold values from -2 to 5, as said below
Outputs:
- weights_block: bfloat16 [768, 768], P(None, 'mp')
- new_master: float32 [768, 768], P('dp', 'mp')
- new_moment: float32 [768, 768], P('dp', 'mp')
- new_second: float32 [768, 768], P('dp', 'mp')
- new_left_stat: float32 [768, 768], P('mp')
- new_right_stat: float32 [768, 768], P('mp')
- new_left_basis: float32 [768, 768], P('mp')
- new_right_basis: float32 [768, 768], P('mp')
Inputs may be any that keep to these rules, and one draw needn't show every extreme that they name: `left_stat`: symmetric. `right_stat`: symmetric.
All inputs are finite; a program needn't handle non-finite values.
Results may differ from a plain program's by a relative error of at most 0.004.
The roundings to bfloat16 on the way count: a program that leaves them out, or rounds other values in their place, can miss the bound.
Values may be sent and summed in bfloat16 or wider, within the bound.
No kernel may reach another device: no remote copies, remote signals or barrier semaphores. Data moves between devices by JAX's collectives and lax.ppermute only.
A program may use at most 64 MiB of HBM per device.

v0:
```python
import jax
import jax.numpy as jnp
from jax import lax
from jax.sharding import PartitionSpec as P

beta_one = 0.9
beta_two = 0.95
beta_stat = 0.95
learn_rate = 0.02
adam_eps = 1e-08
norm_eps = 1e-06
quint_a = 1.875
quint_b = -1.25
quint_c = 0.375
highest = lax.Precision.HIGHEST


def for_sending(x):

    def short(part):
        return part.astype(jnp.bfloat16) if part.dtype == jnp.float32 else part

    return jax.tree.map(short, x)


def all_rows(pair):
    return jax.tree.map(
        lambda part, own: part.astype(own.dtype),
        lax.all_gather(for_sending(pair), "mp", axis=0, tiled=True),
        pair,
    )


def row_gram(row_part, whole_part):
    return lax.dot_general(
        row_part, whole_part, (((1,), (1,)), ((), ())), preferred_element_type=jnp.float32
    )


def scatter_sum(x, axis):
    count = lax.axis_size(axis)
    chunks = x.reshape((count, x.shape[0] // count) + x.shape[1:])
    return jnp.sum(lax.all_to_all(chunks, axis, 0, 0, tiled=False), axis=0)


def gather_rows(x, axis):
    count = lax.axis_size(axis)
    return lax.all_to_all(jnp.broadcast_to(x[None], (count,) + x.shape), axis, 0, 0, tiled=False)


def per_device(micro_grads, master, moment, second, left_basis, right_basis, left_stat, right_stat):
    dp_count = lax.axis_size("dp")
    micro_count = micro_grads.shape[1]
    local_sum = jnp.sum(micro_grads[0], axis=0, dtype=jnp.float32)
    grad_piece = scatter_sum(local_sum, "dp") / (micro_count * dp_count)
    new_moment = beta_one * moment + (1.0 - beta_one) * grad_piece
    pieces = gather_rows(jnp.stack([grad_piece, new_moment]), "dp")
    pieces = jnp.swapaxes(pieces, 0, 1).reshape(2, -1, pieces.shape[-1])
    left_full = lax.all_gather(left_basis, "dp", axis=1, tiled=True)
    both_full = lax.all_gather(pieces, "mp", axis=2, tiled=True)
    right_full = lax.all_gather(right_basis, "mp", axis=1, tiled=True)
    grad_full = both_full[0]
    moment_full = both_full[1]

    def rotate(matrix):
        left_part = lax.dot_general(left_basis, matrix, (((0,), (0,)), ((), ())), precision=highest)
        return jnp.dot(left_part, right_basis, precision=highest)

    rot_grad = rotate(grad_full)
    rot_moment = rotate(moment_full)
    new_second = beta_two * second + (1.0 - beta_two) * rot_grad * rot_grad
    rot_step = rot_moment / (jnp.sqrt(new_second) + adam_eps)
    back_half = scatter_sum(
        lax.dot_general(right_basis, rot_step, (((1,), (1,)), ((), ())), precision=highest), "mp"
    )
    step_piece = scatter_sum(
        lax.dot_general(left_basis, back_half, (((1,), (1,)), ((), ())), precision=highest), "dp"
    )
    new_master = master - learn_rate * step_piece
    weights_block = gather_rows(new_master.astype(jnp.bfloat16), "dp").reshape(
        -1, new_master.shape[1]
    )
    band_width = right_basis.shape[1]
    band_start = lax.axis_index("mp") * band_width
    grad_band = lax.dynamic_slice_in_dim(grad_full, band_start, band_width, 0)
    grad_strip = lax.dynamic_slice_in_dim(grad_full, band_start, band_width, 1)
    left_outer = lax.dot_general(grad_band, grad_full, (((1,), (1,)), ((), ())), precision=highest)
    right_outer = lax.dot_general(
        grad_strip, grad_full, (((0,), (0,)), ((), ())), precision=highest
    )
    new_left_stat = beta_stat * left_stat + (1.0 - beta_stat) * left_outer
    new_right_stat = beta_stat * right_stat + (1.0 - beta_stat) * right_outer
    order_count = left_stat.shape[1]
    power_left = jnp.dot(
        new_left_stat.astype(jnp.bfloat16),
        left_full.astype(jnp.bfloat16),
        preferred_element_type=jnp.float32,
    )
    power_right = jnp.dot(
        new_right_stat.astype(jnp.bfloat16),
        right_full.astype(jnp.bfloat16),
        preferred_element_type=jnp.float32,
    )
    total_left, total_right = lax.psum(
        (jnp.sum(power_left * power_left), jnp.sum(power_right * power_right)), "mp"
    )
    start_left = lax.optimization_barrier(
        (power_left * lax.rsqrt(total_left * (4.0 / order_count) + norm_eps)).astype(jnp.bfloat16)
    )
    start_right = lax.optimization_barrier(
        (power_right * lax.rsqrt(total_right * (4.0 / order_count) + norm_eps)).astype(jnp.bfloat16)
    )
    start_rows = (start_left, start_right)
    start_whole = all_rows(start_rows)
    gram_rows = tuple(
        (
            lax.optimization_barrier(row_gram(row_part, whole_part).astype(jnp.bfloat16))
            for row_part, whole_part in zip(start_rows, start_whole)
        )
    )
    gram_whole = all_rows(gram_rows)
    middle_rows = []
    for row_part, gram_part, gram_all, whole_part in zip(
        start_rows, gram_rows, gram_whole, start_whole
    ):
        square = jnp.dot(gram_part, gram_all, preferred_element_type=jnp.float32)
        poly_rows = (quint_b * gram_part.astype(jnp.float32) + quint_c * square).astype(
            jnp.bfloat16
        )
        middle = quint_a * row_part.astype(jnp.float32) + jnp.dot(
            poly_rows, whole_part, preferred_element_type=jnp.float32
        )
        middle_rows.append(lax.optimization_barrier(middle.astype(jnp.bfloat16)))
    middle_whole = all_rows(tuple(middle_rows))
    new_bases = []
    for row_part, whole_part in zip(middle_rows, middle_whole):
        gram_two = row_gram(row_part, whole_part).astype(jnp.bfloat16)
        new_bases.append(
            1.5 * row_part.astype(jnp.float32)
            - 0.5 * jnp.dot(gram_two, whole_part, preferred_element_type=jnp.float32)
        )
    return (
        weights_block,
        new_master,
        new_moment,
        new_second,
        new_left_stat,
        new_right_stat,
        new_bases[0],
        new_bases[1],
    )


def solution(mesh):
    in_specs = (
        P("dp", None, None, "mp"),
        P("dp", "mp"),
        P("dp", "mp"),
        P("dp", "mp"),
        P(None, "dp"),
        P(None, "mp"),
        P("mp", None),
        P("mp", None),
    )
    out_specs = (
        P(None, "mp"),
        P("dp", "mp"),
        P("dp", "mp"),
        P("dp", "mp"),
        P("mp", None),
        P("mp", None),
        P("mp", None),
        P("mp", None),
    )
    return jax.shard_map(
        per_device, mesh=mesh, in_specs=in_specs, out_specs=out_specs, check_vma=False
    )
```

profile of v0, /device:TPU:2, one launch (start us, length us, event | category | flops | bytes accessed | tf_op | source)
XLA Modules:
  0.0 490.6 jit_solution(16406727266121706216)
XLA Ops:
  7.2 1.4 bitcast_convert_fusion
  8.7 1.0 convert_reduce_fusion
  10.0 31.4 %all_to_all.25 = f32[64,12,96]{2,1,0:T(8,128)S(1)} all-to-all(f32[64,12,96]{2,1,0:T(8,128)S(1)} %reshape.45), channel_id=1, replica_groups=mesh['dp'=64,'mp'=8] {'dp'}, dimensions={0} | all-to-all | bytes 589824 | tf_op jit(solution)/shard_map/all_to_all | solution.py:43
  41.7 28.9 %all_to_all.26 = f32[64,2,12,96]{3,1,2,0:T(2,128)S(1)} all-to-all(f32[64,2,12,96]{3,1,2,0:T(2,128)S(1)} %broadcast_in_dim.4), channel_id=1, replica_groups=mesh['dp'=64,'mp'=8] {'dp'}, dimensions={0} | all-to-all | bytes 1179648 | tf_op jit(solution)/shard_map/all_to_all | solution.py:48
  70.6 1.2 copy.22
  72.7 27.0 %all-gather.27.cloned.1.call-done = bf16[64,12,768]{2,1,0:T(8,128)(2,1)} async-done(((bf16[1,12,768]{2,1,0:T(8,128)(2,1)}), bf16[64,12,768]{2,1,0:T(8,128)(2,1)}) %all-gather.27.cloned.1.call-update) | async-done | bytes 1179664 | tf_op jit(solution)/shard_map/all_gather | solution.py:59
  99.7 3.1 reshape.52
  102.9 59.1 %all-gather.11.cloned.1.call-done = f32[2,768,768]{1,0,2:T(2,128)} async-done(((f32[2,768,96]{1,0,2:T(2,128)}), f32[2,768,768]{1,0,2:T(2,128)}) %all-gather.11.cloned.1.call-update) | async-done | bytes 4718608 | tf_op jit(solution)/shard_map/all_gather | solution.py:60
  162.0 9.3 %fusion.53 = (f32[1,768,768]{1,0,2:T(1,128)S(1)}, f32[1,768,768]{1,0,2:T(1,128)}) fusion(f32[2,768,768]{1,0,2:T(2,128)} %all-gather.11.cloned.1.call-done), kind=kLoop, calls=%fused_computation.70 | loop fusion | bytes 9437184 | tf_op jit(solution)/shard_map/slice | solution.py:62
  171.4 0.9 constant_dynamic-slice_fusion.1
  172.3 1.5 fusion.23
  173.8 1.8 multiply_reduce_fusion.1
  175.7 2.4 fusion.20
  178.1 27.0 %all-gather.19.cloned.1.call-done = bf16[768,768]{0,1:T(8,128)(2,1)} async-done(((bf16[768,96]{0,1:T(8,128)(2,1)}), bf16[768,768]{0,1:T(8,128)(2,1)}) %all-gather.19.cloned.1.call-update) | async-done | bytes 1179664 | tf_op jit(solution)/shard_map/all_gather | solution.py:61
  205.1 2.4 multiply_reduce_fusion
  207.5 16.5 %all-reduce = (f32[]{:T(128)}, f32[]{:T(128)}) all-reduce(f32[]{:T(128)} %get-tuple-element.32, f32[]{:T(128)} %get-tuple-element.34), channel_id=1, replica_groups=mesh['dp'=64,'mp'=8] {'mp'}, use_global_device_ids=true, to_apply=%region_5.0 | all-reduce | flops 2 | bytes 16 | tf_op jit(solution)/shard_map/psum | solution.py:104
  227.0 39.7 %all-gather.21.cloned.1.call-done = bf16[768,768]{1,0:T(8,128)(2,1)} async-done(((bf16[96,768]{1,0:T(8,128)(2,1)}), bf16[768,768]{1,0:T(8,128)(2,1)}) %all-gather.21.cloned.1.call-update) | async-done | bytes 1179664 | tf_op jit(solution)/shard_map/all_gather | solution.py:29
  266.7 2.5 convolution_convert_fusion.1
  269.3 40.1 %all-gather.13.cloned.1.call-done = bf16[768,768]{1,0:T(8,128)(2,1)} async-done(((bf16[96,768]{1,0:T(8,128)(2,1)}), bf16[768,768]{1,0:T(8,128)(2,1)}) %all-gather.13.cloned.1.call-update) | async-done | bytes 1179664 | tf_op jit(solution)/shard_map/all_gather | solution.py:29
  309.5 2.4 convolution_convert_fusion.3
  312.0 40.2 %all-gather.23.cloned.1.call-done = bf16[768,768]{1,0:T(8,128)(2,1)} async-done(((bf16[96,768]{1,0:T(8,128)(2,1)}), bf16[768,768]{1,0:T(8,128)(2,1)}) %all-gather.23.cloned.1.call-update) | async-done | bytes 1179664 | tf_op jit(solution)/shard_map/all_gather | solution.py:29
  352.2 2.9 fusion.33
  355.5 2.0 fusion.4
  357.9 2.0 fusion.6
  359.9 35.2 %all-gather.15.cloned.1.call-done = bf16[768,768]{1,0:T(8,128)(2,1)} async-done(((bf16[96,768]{1,0:T(8,128)(2,1)}), bf16[768,768]{1,0:T(8,128)(2,1)}) %all-gather.15.cloned.1.call-update) | async-done | bytes 1179664 | tf_op jit(solution)/shard_map/all_gather | solution.py:29
  395.1 2.5 fusion.31
  398.4 12.5 %all_to_all.27 = f32[8,96,12]{1,2,0:T(8,128)S(1)} all-to-all(f32[8,96,12]{1,2,0:T(8,128)S(1)} %copy.23), channel_id=1, replica_groups=mesh['dp'=64,'mp'=8] {'mp'}, dimensions={0} | all-to-all | bytes 73728 | tf_op jit(solution)/shard_map/all_to_all | solution.py:43
  411.6 28.3 %all_to_all.28 = f32[64,12,96]{2,1,0:T(8,128)S(1)} all-to-all(f32[64,12,96]{2,1,0:T(8,128)S(1)} %reshape.48), channel_id=1, replica_groups=mesh['dp'=64,'mp'=8] {'dp'}, dimensions={0} | all-to-all | bytes 589824 | tf_op jit(solution)/shard_map/all_to_all | solution.py:43
  440.6 17.9 %all_to_all.29 = bf16[64,12,96]{2,1,0:T(8,128)(2,1)S(1)} all-to-all(bf16[64,12,96]{2,1,0:T(8,128)(2,1)S(1)} %broadcast_in_dim.5), channel_id=1, replica_groups=mesh['dp'=64,'mp'=8] {'dp'}, dimensions={0} | all-to-all | bytes 294912 | tf_op jit(solution)/shard_map/all_to_all | solution.py:48
  459.4 3.1 fusion.26
  462.5 18.4 %all-gather.17.cloned.1.call-done = bf16[768,768]{1,0:T(8,128)(2,1)} async-done(((bf16[96,768]{1,0:T(8,128)(2,1)}), bf16[768,768]{1,0:T(8,128)(2,1)}) %all-gather.17.cloned.1.call-update) | async-done | bytes 1179664 | tf_op jit(solution)/shard_map/all_gather | solution.py:29
  480.9 3.1 fusion.28
  (86 shorter events, 7.0 us)
Async XLA Ops:
  7.2 92.6 %all-gather.27.cloned.1.call-start = ((), (), s32[]{:S(2)}) async-start(), calls=%async_computation.13 | async-start | bytes 1597440 | tf_op jit(solution)/shard_map/all_gather | solution.py:59
  8.6 153.4 %all-gather.11.cloned.1.call-start = ((), (), s32[]{:S(2)}) async-start(), calls=%async_computation.5 | async-start | bytes 5308416 | tf_op jit(solution)/shard_map/all_gather | solution.py:60
  9.9 31.5 %copy-start.20 = (f32[12,96]{1,0:T(8,128)S(1)}, f32[12,96]{1,0:T(8,128)}, u32[]{:S(2)}) copy-start(f32[12,96]{1,0:T(8,128)} %param.10) | copy-start | bytes 13828
  41.4 29.1 %copy-start.17 = (f32[12,96]{1,0:T(8,128)}, f32[12,96]{1,0:T(8,128)S(1)}, u32[]{:S(2)}) copy-start(f32[12,96]{1,0:T(8,128)S(1)} %get-tuple-element.31) | copy-start | bytes 13828
  70.6 1.2 copy-start.1
  71.7 133.4 %all-gather.19.cloned.1.call-start = ((), (), s32[]{:S(2)}) async-start(), calls=%async_computation.9 | async-start | bytes 1327104 | tf_op jit(solution)/shard_map/all_gather | solution.py:61
  72.5 194.2 %all-gather.21.cloned.1.call-start = ((), (), s32[]{:S(2)}) async-start(), calls=%async_computation.10 | async-start | bytes 1327104 | tf_op jit(solution)/shard_map/all_gather | solution.py:29
  171.3 1.0 copy-start.14
  172.3 1.6 copy-start.3
  173.8 4.2 copy-start.10
  173.8 1.8 copy-start.15
  178.1 47.4 %copy-start.11 = (f32[96,768]{1,0:T(8,128)}, f32[96,768]{1,0:T(8,128)S(1)}, u32[]{:S(2)}) copy-start(f32[96,768]{1,0:T(8,128)S(1)} %fusion.20) | copy-start | bytes 884740
  205.1 21.1 %copy-start.12 = (f32[96,768]{1,0:T(8,128)S(1)}, f32[96,768]{1,0:T(8,128)}, u32[]{:S(2)}) copy-start(f32[96,768]{1,0:T(8,128)} %get-tuple-element.33) | copy-start | bytes 884740
  225.5 84.0 %all-gather.13.cloned.1.call-start = ((), (), s32[]{:S(2)}) async-start(), calls=%async_computation.6 | async-start | bytes 1327104 | tf_op jit(solution)/shard_map/all_gather | solution.py:29
  226.9 82.6 %copy-start.4 = (bf16[96,768]{1,0:T(8,128)(2,1)S(1)}, bf16[96,768]{1,0:T(8,128)(2,1)}, u32[]{:S(2)}) copy-start(bf16[96,768]{1,0:T(8,128)(2,1)} %multiply_convert_fusion.1) | copy-start | bytes 442372
  226.9 125.3 %all-gather.23.cloned.1.call-start = ((), (), s32[]{:S(2)}) async-start(), calls=%async_computation.11 | async-start | bytes 1327104 | tf_op jit(solution)/shard_map/all_gather | solution.py:29
  269.2 83.0 %copy-start.5 = (bf16[96,768]{1,0:T(8,128)(2,1)S(1)}, bf16[96,768]{1,0:T(8,128)(2,1)}, u32[]{:S(2)}) copy-start(bf16[96,768]{1,0:T(8,128)(2,1)} %multiply_convert_fusion) | copy-start | bytes 442372
  269.3 83.0 %copy-start.9 = (bf16[96,768]{1,0:T(8,128)(2,1)S(1)}, bf16[96,768]{1,0:T(8,128)(2,1)}, u32[]{:S(2)}) copy-start(bf16[96,768]{1,0:T(8,128)(2,1)} %convolution_convert_fusion.1) | copy-start | bytes 442372
  269.3 125.9 %all-gather.15.cloned.1.call-start = ((), (), s32[]{:S(2)}) async-start(), calls=%async_computation.7 | async-start | bytes 1327104 | tf_op jit(solution)/shard_map/all_gather | solution.py:29
  311.9 43.5 %copy-start.13 = (f32[768,12]{0,1:T(8,128)S(1)}, f32[768,12]{0,1:T(8,128)}, u32[]{:S(2)}) copy-start(f32[768,12]{0,1:T(8,128)} %param.12) | copy-start | bytes 110596
  312.0 147.4 %all-gather.25.cloned.1.call-start = ((), (), s32[]{:S(2)}) async-start(), calls=%async_computation.12 | async-start | bytes 1327104 | tf_op jit(solution)/shard_map/all_gather | solution.py:29
  355.2 2.4 copy-start.18
  355.2 125.8 %all-gather.17.cloned.1.call-start = ((), (), s32[]{:S(2)}) async-start(), calls=%async_computation.8 | async-start | bytes 1327104 | tf_op jit(solution)/shard_map/all_gather | solution.py:29
  355.4 2.4 copy-start
  357.8 39.9 %copy-start.16 = (f32[12,96]{1,0:T(8,128)}, f32[12,96]{1,0:T(8,128)S(1)}, u32[]{:S(2)}) copy-start(f32[12,96]{1,0:T(8,128)S(1)} %fusion.47) | copy-start | bytes 13828
  357.9 37.3 %copy-start.2 = (bf16[768,768]{1,0:T(8,128)(2,1)S(1)}, bf16[768,768]{1,0:T(8,128)(2,1)}, u32[]{:S(2)}) copy-start(bf16[768,768]{1,0:T(8,128)(2,1)} %all-gather.13.cloned.1.call-done) | copy-start | bytes 3538948
  357.9 37.2 %copy-start.8 = (bf16[96,768]{1,0:T(8,128)(2,1)S(1)}, bf16[96,768]{1,0:T(8,128)(2,1)}, u32[]{:S(2)}) copy-start(bf16[96,768]{1,0:T(8,128)(2,1)} %convolution_convert_fusion.3) | copy-start | bytes 442372
  411.5 28.4 %copy-start.19 = (f32[12,96]{1,0:T(8,128)S(1)}, f32[12,96]{1,0:T(8,128)}, u32[]{:S(2)}) copy-start(f32[12,96]{1,0:T(8,128)} %param.9) | copy-start | bytes 13828
  439.8 19.5 %copy-start.6 = (bf16[96,768]{1,0:T(8,128)(2,1)S(1)}, bf16[96,768]{1,0:T(8,128)(2,1)}, u32[]{:S(2)}) copy-start(bf16[96,768]{1,0:T(8,128)(2,1)} %fusion.33) | copy-start | bytes 442372
  459.4 21.5 %copy-start.7 = (bf16[96,768]{1,0:T(8,128)(2,1)S(1)}, bf16[96,768]{1,0:T(8,128)(2,1)}, u32[]{:S(2)}) copy-start(bf16[96,768]{1,0:T(8,128)(2,1)} %fusion.31) | copy-start | bytes 442372
Sparse Core Ops, SparseCore 0:
  11.9 87.7 all-gather.26
  101.8 60.1 all-gather.10
  164.7 40.3 all-gather.18
  225.6 41.0 all-gather.20
  269.2 40.2 all-gather.12
  312.0 40.2 all-gather.22
  354.9 40.2 all-gather.14
  397.8 40.2 all-gather.24
  440.7 40.1 all-gather.16
where the time goes:
time: 491 us
  waiting for transfers between devices  287 us (58%)
  blocking collectives  135 us (27%)
  matrix products  30.2 us (6%)
  local copies, waits for them, and re-layouts  16.3 us (3%)
  between operations  15.6 us (3%)
  other arithmetic  5.29 us (1%)
    all_gather x6, waiting for transfers between devices, all_rows(): lax.all_gather(for_sending(pair), 'mp', axis=0, tiled=True)  174 us
    all_to_all x3, blocking collectives, scatter_sum(): return jnp.sum(lax.all_to_all(chunks, axis, 0, 0, tiled=False), axis=0)  72.1 us
    all_gather x1, waiting for transfers between devices, per_device(): both_full = lax.all_gather(pieces, 'mp', axis=2, tiled=True)  59.1 us
    all_to_all x2, blocking collectives, gather_rows(): lax.all_to_all(jnp.broadcast_to(x[None], (count,) + x.shape), axis, 0, 0,...  46.8 us
    all_gather x1, waiting for transfers between devices, per_device(): right_full = lax.all_gather(right_basis, 'mp', axis=1, tiled=True)  27 us
    all_gather x1, waiting for transfers between devices, per_device(): left_full = lax.all_gather(left_basis, 'dp', axis=1, tiled=True)  27 us
    psum x1, blocking collectives, per_device(): lax.psum((jnp.sum(power_left * power_left), jnp.sum(power_right * power_r...  16.5 us
  transfers between devices with their start and end apart: 9, of which 8 were waited for; matrix products, arithmetic and copies ran while one was open for 9% of the time, Pallas kernels for 0%

commit v1 on v0

--- a/solution.py
+++ b/solution.py
@@ -13,6 +13,17 @@
 quint_b = -1.25
 quint_c = 0.375
 highest = lax.Precision.HIGHEST
+
+
+def around_the_ring(shard, name, dim):
+    size = lax.axis_size(name)
+    right = [(i, (i + 1) % size) for i in range(size)]
+    pieces = [shard]
+    for far in range(1, size):
+        pieces = [lax.ppermute(pieces[0], name, right), *pieces]
+    out = jnp.concatenate(pieces, axis=dim)
+    shift = (lax.axis_index(name) + 1) * pieces[-1].shape[dim]
+    return jnp.roll(out, shift, axis=dim)
 
 
 def for_sending(x):
@@ -58,7 +69,7 @@
     pieces = jnp.swapaxes(pieces, 0, 1).reshape(2, -1, pieces.shape[-1])
     left_full = lax.all_gather(left_basis, "dp", axis=1, tiled=True)
     both_full = lax.all_gather(pieces, "mp", axis=2, tiled=True)
-    right_full = lax.all_gather(right_basis, "mp", axis=1, tiled=True)
+    right_full = around_the_ring(right_basis, "mp", 1)
     grad_full = both_full[0]
     moment_full = both_full[1]
 

time: 491 us -> 466 us (0.949)
  waiting for transfers between devices: 287 us -> 236 us
  starting transfers between devices: 0.77 us -> 15.6 us
  local copies, waits for them, and re-layouts: 16.3 us -> 27.1 us
    ppermute x0 -> x7, waiting for transfers between devices: none -> 50.7 us  [around_the_ring(): pieces = [lax.ppermute(pieces[0], name, right), *pieces]]
    all_gather x1, waiting for transfers between devices: 59.1 us -> 15.1 us  [per_device(): both_full = lax.all_gather(pieces, 'mp', axis=2, tiled=True)]
    all_gather x1 -> x0, waiting for transfers between devices: 27 us -> none  [per_device(): right_full = lax.all_gather(right_basis, 'mp', axis=1, tiled=True)]
    all_gather x1, waiting for transfers between devices: 27 us -> 0.01 us  [per_device(): left_full = lax.all_gather(left_basis, 'dp', axis=1, tiled=True)]
    ppermute x0 -> x7, starting transfers between devices: none -> 15.1 us  [around_the_ring(): pieces = [lax.ppermute(pieces[0], name, right), *pieces]]
    unnamed x43 -> x54, local copies, waits for them, and re-layouts: 0.96 us -> 11 us
  transfers between devices with their start and end apart: 9 -> 15, of which waited for: 8 -> 13; matrix products, arithmetic and copies ran while one was open for 9% -> 8% of each run, Pallas kernels for 0% -> 0%
where the time goes in v1:
time: 466 us; the launch traced here: 465 us
  waiting for transfers between devices  236 us (51%)
  blocking collectives  135 us (29%)
  matrix products  30.3 us (7%)
  local copies, waits for them, and re-layouts  27.1 us (6%)
  between operations  15.9 us (3%)
  starting transfers between devices  15.6 us (3%)
  other arithmetic  5.58 us (1%)
    all_gather x6, waiting for transfers between devices, all_rows(): lax.all_gather(for_sending(pair), 'mp', axis=0, tiled=True)  170 us
    all_to_all x3, blocking collectives, scatter_sum(): return jnp.sum(lax.all_to_all(chunks, axis, 0, 0, tiled=False), axis=0)  72.1 us
    ppermute x7, waiting for transfers between devices, around_the_ring(): pieces = [lax.ppermute(pieces[0], name, right), *pieces]  50.7 us
    all_to_all x2, blocking collectives, gather_rows(): lax.all_to_all(jnp.broadcast_to(x[None], (count,) + x.shape), axis, 0, 0,...  46.8 us
    psum x1, blocking collectives, per_device(): lax.psum((jnp.sum(power_left * power_left), jnp.sum(power_right * power_r...  16.1 us
    all_gather x1, waiting for transfers between devices, per_device(): both_full = lax.all_gather(pieces, 'mp', axis=2, tiled=True)  15.1 us
    ppermute x7, starting transfers between devices, around_the_ring(): pieces = [lax.ppermute(pieces[0], name, right), *pieces]  15.1 us
    unnamed x54, local copies, waits for them, and re-layouts  11 us
  transfers between devices with their start and end apart: 15, of which 13 were waited for; matrix products, arithmetic and copies ran while one was open for 8% of the time, Pallas kernels for 0%

profile of v1, /device:TPU:2, one launch (start us, length us, event | category | flops | bytes accessed | tf_op | source)
XLA Modules:
  0.0 465.3 jit_solution(16331814602641515880)
XLA Ops:
  10.0 31.4 %all_to_all.25 = f32[64,12,96]{2,1,0:T(8,128)S(1)} all-to-all(f32[64,12,96]{2,1,0:T(8,128)S(1)} %reshape.45), channel_id=1, replica_groups=mesh['dp'=64,'mp'=8] {'dp'}, dimensions={0} | all-to-all | bytes 589824 | tf_op jit(solution)/shard_map/all_to_all | solution.py:54
  41.7 28.9 %all_to_all.26 = f32[64,2,12,96]{3,1,2,0:T(2,128)S(1)} all-to-all(f32[64,2,12,96]{3,1,2,0:T(2,128)S(1)} %broadcast_in_dim.4), channel_id=1, replica_groups=mesh['dp'=64,'mp'=8] {'dp'}, dimensions={0} | all-to-all | bytes 1179648 | tf_op jit(solution)/shard_map/all_to_all | solution.py:59
  71.8 3.5 collective-permute-start
  75.3 5.3 %collective-permute-done = bf16[768,96]{0,1:T(8,128)(2,1)S(1)} collective-permute-done((bf16[768,96]{0,1:T(8,128)(2,1)S(1)}, bf16[768,96]{0,1:T(8,128)(2,1)S(1)}, u32[]{:S(2)}, u32[]{:S(2)}) %collective-permute-start) | collective-permute-done | bytes 147488 | tf_op jit(solution)/shard_map/ppermute | solution.py:23
  82.5 6.3 %collective-permute-done.1 = bf16[768,96]{0,1:T(8,128)(2,1)S(1)} collective-permute-done((bf16[768,96]{0,1:T(8,128)(2,1)S(1)}, bf16[768,96]{0,1:T(8,128)(2,1)S(1)}, u32[]{:S(2)}, u32[]{:S(2)}) %collective-permute-start.1) | collective-permute-done | bytes 147488 | tf_op jit(solution)/shard_map/ppermute | solution.py:23
  90.7 6.3 %collective-permute-done.2 = bf16[768,96]{0,1:T(8,128)(2,1)S(1)} collective-permute-done((bf16[768,96]{0,1:T(8,128)(2,1)S(1)}, bf16[768,96]{0,1:T(8,128)(2,1)S(1)}, u32[]{:S(2)}, u32[]{:S(2)}) %collective-permute-start.2) | collective-permute-done | bytes 147488 | tf_op jit(solution)/shard_map/ppermute | solution.py:23
  98.9 6.3 %collective-permute-done.3 = bf16[768,96]{0,1:T(8,128)(2,1)S(1)} collective-permute-done((bf16[768,96]{0,1:T(8,128)(2,1)S(1)}, bf16[768,96]{0,1:T(8,128)(2,1)S(1)}, u32[]{:S(2)}, u32[]{:S(2)}) %collective-permute-start.3) | collective-permute-done | bytes 147488 | tf_op jit(solution)/shard_map/ppermute | solution.py:23
  107.2 6.3 %collective-permute-done.4 = bf16[768,96]{0,1:T(8,128)(2,1)S(1)} collective-permute-done((bf16[768,96]{0,1:T(8,128)(2,1)S(1)}, bf16[768,96]{0,1:T(8,128)(2,1)S(1)}, u32[]{:S(2)}, u32[]{:S(2)}) %collective-permute-start.4) | collective-permute-done | bytes 147488 | tf_op jit(solution)/shard_map/ppermute | solution.py:23
  115.4 10.9 %collective-permute-done.5 = bf16[768,96]{0,1:T(8,128)(2,1)S(1)} collective-permute-done((bf16[768,96]{0,1:T(8,128)(2,1)S(1)}, bf16[768,96]{0,1:T(8,128)(2,1)S(1)}, u32[]{:S(2)}, u32[]{:S(2)}) %collective-permute-start.5) | collective-permute-done | bytes 147488 | tf_op jit(solution)/shard_map/ppermute | solution.py:23
  126.3 2.1 collective-permute-start.6
  128.4 9.2 %collective-permute-done.6 = bf16[768,96]{0,1:T(8,128)(2,1)S(1)} collective-permute-done((bf16[768,96]{0,1:T(8,128)(2,1)S(1)}, bf16[768,96]{0,1:T(8,128)(2,1)S(1)}, u32[]{:S(2)}, u32[]{:S(2)}) %collective-permute-start.6) | collective-permute-done | bytes 147488 | tf_op jit(solution)/shard_map/ppermute | solution.py:23
  148.4 3.2 reshape.52
  151.6 15.1 %all-gather.10.cloned.1.call-done = f32[2,768,768]{1,0,2:T(2,128)} async-done(((f32[2,768,96]{1,0,2:T(2,128)}), f32[2,768,768]{1,0,2:T(2,128)}) %all-gather.10.cloned.1.call-update) | async-done | bytes 4718608 | tf_op jit(solution)/shard_map/all_gather | solution.py:71
  166.8 9.3 %fusion.53 = (f32[1,768,768]{1,0,2:T(1,128)S(1)}, f32[1,768,768]{1,0,2:T(1,128)}) fusion(f32[2,768,768]{1,0,2:T(2,128)} %all-gather.10.cloned.1.call-done), kind=kLoop, calls=%fused_computation.87 | loop fusion | bytes 9437184 | tf_op jit(solution)/shard_map/slice | solution.py:73
  178.6 2.4 fusion.19
  182.1 3.1 multiply_reduce_fusion
  185.2 16.1 %all-reduce = (f32[]{:T(128)}, f32[]{:T(128)}) all-reduce(f32[]{:T(128)} %get-tuple-element.32, f32[]{:T(128)} %get-tuple-element.34), channel_id=1, replica_groups=mesh['dp'=64,'mp'=8] {'mp'}, use_global_device_ids=true, to_apply=%region_5.6 | all-reduce | flops 2 | bytes 16 | tf_op jit(solution)/shard_map/psum | solution.py:115
  205.2 37.3 %all-gather.12.cloned.1.call-done = bf16[768,768]{1,0:T(8,128)(2,1)} async-done(((bf16[96,768]{1,0:T(8,128)(2,1)}), bf16[768,768]{1,0:T(8,128)(2,1)}) %all-gather.12.cloned.1.call-update) | async-done | bytes 1179664 | tf_op jit(solution)/shard_map/all_gather | solution.py:40
  242.5 2.5 convolution_convert_fusion.3
  245.1 39.6 %all-gather.18.cloned.1.call-done = bf16[768,768]{1,0:T(8,128)(2,1)} async-done(((bf16[96,768]{1,0:T(8,128)(2,1)}), bf16[768,768]{1,0:T(8,128)(2,1)}) %all-gather.18.cloned.1.call-update) | async-done | bytes 1179664 | tf_op jit(solution)/shard_map/all_gather | solution.py:40
  284.7 2.5 convolution_convert_fusion.1
  287.3 40.1 %all-gather.14.cloned.1.call-done = bf16[768,768]{1,0:T(8,128)(2,1)} async-done(((bf16[96,768]{1,0:T(8,128)(2,1)}), bf16[768,768]{1,0:T(8,128)(2,1)}) %all-gather.14.cloned.1.call-update) | async-done | bytes 1179664 | tf_op jit(solution)/shard_map/all_gather | solution.py:40
  327.4 3.0 fusion.30
  330.7 2.0 fusion.4
  335.2 34.4 %all-gather.20.cloned.1.call-done = bf16[768,768]{1,0:T(8,128)(2,1)} async-done(((bf16[96,768]{1,0:T(8,128)(2,1)}), bf16[768,768]{1,0:T(8,128)(2,1)}) %all-gather.20.cloned.1.call-update) | async-done | bytes 1179664 | tf_op jit(solution)/shard_map/all_gather | solution.py:40
  369.6 2.5 fusion.32
  372.9 12.5 %all_to_all.27 = f32[8,96,12]{1,2,0:T(8,128)S(1)} all-to-all(f32[8,96,12]{1,2,0:T(8,128)S(1)} %copy.23), channel_id=1, replica_groups=mesh['dp'=64,'mp'=8] {'mp'}, dimensions={0} | all-to-all | bytes 73728 | tf_op jit(solution)/shard_map/all_to_all | solution.py:54
  386.1 28.3 %all_to_all.28 = f32[64,12,96]{2,1,0:T(8,128)S(1)} all-to-all(f32[64,12,96]{2,1,0:T(8,128)S(1)} %reshape.48), channel_id=1, replica_groups=mesh['dp'=64,'mp'=8] {'dp'}, dimensions={0} | all-to-all | bytes 589824 | tf_op jit(solution)/shard_map/all_to_all | solution.py:54
  415.1 17.9 %all_to_all.29 = bf16[64,12,96]{2,1,0:T(8,128)(2,1)S(1)} all-to-all(bf16[64,12,96]{2,1,0:T(8,128)(2,1)S(1)} %broadcast_in_dim.5), channel_id=1, replica_groups=mesh['dp'=64,'mp'=8] {'dp'}, dimensions={0} | all-to-all | bytes 294912 | tf_op jit(solution)/shard_map/all_to_all | solution.py:59
  433.9 3.1 fusion.27
  437.0 18.4 %all-gather.22.cloned.1.call-done = bf16[768,768]{1,0:T(8,128)(2,1)} async-done(((bf16[96,768]{1,0:T(8,128)(2,1)}), bf16[768,768]{1,0:T(8,128)(2,1)}) %all-gather.22.cloned.1.call-update) | async-done | bytes 1179664 | tf_op jit(solution)/shard_map/all_gather | solution.py:40
  455.4 3.1 fusion.25
  (109 shorter events, 36.5 us)
Async XLA Ops:
  7.2 34.2 %copy-start.18 = (f32[12,96]{1,0:T(8,128)S(1)}, f32[12,96]{1,0:T(8,128)}, u32[]{:S(2)}) copy-start(f32[12,96]{1,0:T(8,128)} %param.10) | copy-start | bytes 13828
  7.2 141.3 %all-gather.24.cloned.1.call-start = ((), (), s32[]{:S(2)}) async-start(), calls=%async_computation.12 | async-start | bytes 1597440 | tf_op jit(solution)/shard_map/all_gather | solution.py:70
  8.7 158.1 %all-gather.10.cloned.1.call-start = ((), (), s32[]{:S(2)}) async-start(), calls=%async_computation.5 | async-start | bytes 5308416 | tf_op jit(solution)/shard_map/all_gather | solution.py:71
  41.3 30.5 %copy-start = (f32[768,96]{0,1:T(8,128)S(1)}, f32[768,96]{0,1:T(8,128)}, u32[]{:S(2)}) copy-start(f32[768,96]{0,1:T(8,128)} %param.13) | copy-start | bytes 884740
  41.4 30.4 %copy-start.15 = (f32[12,96]{1,0:T(8,128)}, f32[12,96]{1,0:T(8,128)S(1)}, u32[]{:S(2)}) copy-start(f32[12,96]{1,0:T(8,128)S(1)} %get-tuple-element.31) | copy-start | bytes 13828
  71.7 170.8 %all-gather.12.cloned.1.call-start = ((), (), s32[]{:S(2)}) async-start(), calls=%async_computation.6 | async-start | bytes 1327104 | tf_op jit(solution)/shard_map/all_gather | solution.py:40
  71.8 8.7 %collective-permute-start = (bf16[768,96]{0,1:T(8,128)(2,1)S(1)}, bf16[768,96]{0,1:T(8,128)(2,1)S(1)}, u32[]{:S(2)}, u32[]{:S(2)}) collective-permute-start(bf16[768,96]{0,1:T(8,128)(2,1)S(1)} %convert.2), channel_id=1, source_target_pairs={{0,1},{1,2},{2,3},{3,4},{4,5},{5,6},{6,7},{7,0},{8,9},{9,10},{10,1... | collective-permute-start | bytes 442376 | tf_op jit(solution)/shard_map/ppermute | solution.py:23
  80.5 8.2 %collective-permute-start.1 = (bf16[768,96]{0,1:T(8,128)(2,1)S(1)}, bf16[768,96]{0,1:T(8,128)(2,1)S(1)}, u32[]{:S(2)}, u32[]{:S(2)}) collective-permute-start(bf16[768,96]{0,1:T(8,128)(2,1)S(1)} %collective-permute-done), channel_id=1, source_target_pairs={{0,1},{1,2},{2,3},{3,4},{4,5},{5,6},{6,7},{7,0},{8,9},{9,10},{10,1... | collective-permute-start | bytes 442376 | tf_op jit(solution)/shard_map/ppermute | solution.py:23
  88.8 8.2 %collective-permute-start.2 = (bf16[768,96]{0,1:T(8,128)(2,1)S(1)}, bf16[768,96]{0,1:T(8,128)(2,1)S(1)}, u32[]{:S(2)}, u32[]{:S(2)}) collective-permute-start(bf16[768,96]{0,1:T(8,128)(2,1)S(1)} %collective-permute-done.1), channel_id=1, source_target_pairs={{0,1},{1,2},{2,3},{3,4},{4,5},{5,6},{6,7},{7,0},{8,9},{9,10},{10,1... | collective-permute-start | bytes 442376 | tf_op jit(solution)/shard_map/ppermute | solution.py:23
  97.0 8.2 %collective-permute-start.3 = (bf16[768,96]{0,1:T(8,128)(2,1)S(1)}, bf16[768,96]{0,1:T(8,128)(2,1)S(1)}, u32[]{:S(2)}, u32[]{:S(2)}) collective-permute-start(bf16[768,96]{0,1:T(8,128)(2,1)S(1)} %collective-permute-done.2), channel_id=1, source_target_pairs={{0,1},{1,2},{2,3},{3,4},{4,5},{5,6},{6,7},{7,0},{8,9},{9,10},{10,1... | collective-permute-start | bytes 442376 | tf_op jit(solution)/shard_map/ppermute | solution.py:23
  105.2 8.2 %collective-permute-start.4 = (bf16[768,96]{0,1:T(8,128)(2,1)S(1)}, bf16[768,96]{0,1:T(8,128)(2,1)S(1)}, u32[]{:S(2)}, u32[]{:S(2)}) collective-permute-start(bf16[768,96]{0,1:T(8,128)(2,1)S(1)} %collective-permute-done.3), channel_id=1, source_target_pairs={{0,1},{1,2},{2,3},{3,4},{4,5},{5,6},{6,7},{7,0},{8,9},{9,10},{10,1... | collective-permute-start | bytes 442376 | tf_op jit(solution)/shard_map/ppermute | solution.py:23
  113.5 12.8 %collective-permute-start.5 = (bf16[768,96]{0,1:T(8,128)(2,1)S(1)}, bf16[768,96]{0,1:T(8,128)(2,1)S(1)}, u32[]{:S(2)}, u32[]{:S(2)}) collective-permute-start(bf16[768,96]{0,1:T(8,128)(2,1)S(1)} %collective-permute-done.4), channel_id=1, source_target_pairs={{0,1},{1,2},{2,3},{3,4},{4,5},{5,6},{6,7},{7,0},{8,9},{9,10},{10,1... | collective-permute-start | bytes 442376 | tf_op jit(solution)/shard_map/ppermute | solution.py:23
  126.3 11.4 %collective-permute-start.6 = (bf16[768,96]{0,1:T(8,128)(2,1)S(1)}, bf16[768,96]{0,1:T(8,128)(2,1)S(1)}, u32[]{:S(2)}, u32[]{:S(2)}) collective-permute-start(bf16[768,96]{0,1:T(8,128)(2,1)S(1)} %collective-permute-done.5), channel_id=1, source_target_pairs={{0,1},{1,2},{2,3},{3,4},{4,5},{5,6},{6,7},{7,0},{8,9},{9,10},{10,1... | collective-permute-start | bytes 442376 | tf_op jit(solution)/shard_map/ppermute | solution.py:23
  151.6 25.4 %copy-start.12 = (f32[96,768]{1,0:T(8,128)S(1)}, f32[96,768]{1,0:T(8,128)}, u32[]{:S(2)}) copy-start(f32[96,768]{1,0:T(8,128)} %param.14) | copy-start | bytes 884740
  176.0 2.5 copy-start.13
  178.6 3.6 copy-start.9
  181.0 24.1 %copy-start.10 = (f32[96,768]{1,0:T(8,128)}, f32[96,768]{1,0:T(8,128)S(1)}, u32[]{:S(2)}) copy-start(f32[96,768]{1,0:T(8,128)S(1)} %fusion.19) | copy-start | bytes 884740
  202.7 124.7 %copy-start.5 = (bf16[96,768]{1,0:T(8,128)(2,1)S(1)}, bf16[96,768]{1,0:T(8,128)(2,1)}, u32[]{:S(2)}) copy-start(bf16[96,768]{1,0:T(8,128)(2,1)} %multiply_convert_fusion.1) | copy-start | bytes 442372
  202.7 81.9 %all-gather.18.cloned.1.call-start = ((), (), s32[]{:S(2)}) async-start(), calls=%async_computation.9 | async-start | bytes 1327104 | tf_op jit(solution)/shard_map/all_gather | solution.py:40
  205.1 122.3 %all-gather.14.cloned.1.call-start = ((), (), s32[]{:S(2)}) async-start(), calls=%async_computation.7 | async-start | bytes 1327104 | tf_op jit(solution)/shard_map/all_gather | solution.py:40
  245.0 85.7 %copy-start.11 = (f32[768,12]{0,1:T(8,128)S(1)}, f32[768,12]{0,1:T(8,128)}, u32[]{:S(2)}) copy-start(f32[768,12]{0,1:T(8,128)} %param.12) | copy-start | bytes 110596
  245.0 124.6 %all-gather.20.cloned.1.call-start = ((), (), s32[]{:S(2)}) async-start(), calls=%async_computation.10 | async-start | bytes 1327104 | tf_op jit(solution)/shard_map/all_gather | solution.py:40
  287.2 45.6 %copy-start.16 = (f32[12,96]{1,0:T(8,128)S(1)}, f32[12,96]{1,0:T(8,128)}, u32[]{:S(2)}) copy-start(f32[12,96]{1,0:T(8,128)} %param.11) | copy-start | bytes 13828
  287.2 146.6 %all-gather.16.cloned.1.call-start = ((), (), s32[]{:S(2)}) async-start(), calls=%async_computation.8 | async-start | bytes 1327104 | tf_op jit(solution)/shard_map/all_gather | solution.py:40
  330.4 39.2 %copy-start.4 = (bf16[96,768]{1,0:T(8,128)(2,1)S(1)}, bf16[96,768]{1,0:T(8,128)(2,1)}, u32[]{:S(2)}) copy-start(bf16[96,768]{1,0:T(8,128)(2,1)} %multiply_convert_fusion) | copy-start | bytes 442372
  330.4 39.2 %copy-start.8 = (bf16[96,768]{1,0:T(8,128)(2,1)S(1)}, bf16[96,768]{1,0:T(8,128)(2,1)}, u32[]{:S(2)}) copy-start(bf16[96,768]{1,0:T(8,128)(2,1)} %convolution_convert_fusion.1) | copy-start | bytes 442372
  330.4 124.9 %all-gather.22.cloned.1.call-start = ((), (), s32[]{:S(2)}) async-start(), calls=%async_computation.11 | async-start | bytes 1327104 | tf_op jit(solution)/shard_map/all_gather | solution.py:40
  332.8 36.8 %copy-start.2 = (bf16[768,768]{1,0:T(8,128)(2,1)S(1)}, bf16[768,768]{1,0:T(8,128)(2,1)}, u32[]{:S(2)}) copy-start(bf16[768,768]{1,0:T(8,128)(2,1)} %all-gather.18.cloned.1.call-done) | copy-start | bytes 3538948
  333.1 39.1 %copy-start.14 = (f32[12,96]{1,0:T(8,128)}, f32[12,96]{1,0:T(8,128)S(1)}, u32[]{:S(2)}) copy-start(f32[12,96]{1,0:T(8,128)S(1)} %fusion.46) | copy-start | bytes 13828
  372.2 42.2 %copy-start.17 = (f32[12,96]{1,0:T(8,128)S(1)}, f32[12,96]{1,0:T(8,128)}, u32[]{:S(2)}) copy-start(f32[12,96]{1,0:T(8,128)} %param.9) | copy-start | bytes 13828
  385.8 48.0 %copy-start.6 = (bf16[96,768]{1,0:T(8,128)(2,1)S(1)}, bf16[96,768]{1,0:T(8,128)(2,1)}, u32[]{:S(2)}) copy-start(bf16[96,768]{1,0:T(8,128)(2,1)} %fusion.30) | copy-start | bytes 442372
  414.3 41.0 %copy-start.7 = (bf16[96,768]{1,0:T(8,128)(2,1)S(1)}, bf16[96,768]{1,0:T(8,128)(2,1)}, u32[]{:S(2)}) copy-start(bf16[96,768]{1,0:T(8,128)(2,1)} %fusion.32) | copy-start | bytes 442372
  (2 other events, 4.8 us)
Sparse Core Ops, SparseCore 0:
  11.9 87.7 all-gather.23
  101.8 64.9 all-gather.9
  202.8 39.5 all-gather.11
  244.4 40.2 all-gather.17
  287.2 40.2 all-gather.13
  329.3 40.2 all-gather.19
  372.2 40.2 all-gather.15
  415.1 40.1 all-gather.21
